TPU v7x, 128 devices: a whole 4x4x4 slice. The times are simulated.
128 devices in a mesh: ep: 32 (over z, x, core), tp: 4 (over y).
Axes of the slice: x: 4, y: 4, z: 4, core: 2. Of those that a mesh axis runs over, the one named last changes fastest.
Arguments:
- stream: bfloat16 [16384, 2048], P('ep'), may hold values from -6 to 6
- queries: bfloat16 [16384, 2048], P('ep', 'tp'), may hold values from -6 to 6
- keys_in: bfloat16 [16384, 2048], P('ep', 'tp'), may hold values from -6 to 6
- values_in: bfloat16 [16384, 2048], P('ep', 'tp'), may hold values from -6 to 6
- segment_ids: int32 [32, 512], P('ep'), may hold values from 0 to 5, never falling along the last dimension, each value on 1 to 256 neighbouring positions
- routes: int32 [16384, 4], P('ep'), may hold values from 0 to 63, all different within a row; in each aligned block of 512 rows (0 to 511, 512 to 1023, ...) at most 48 rows name the same one
- route_weights: float32 [16384, 4], P('ep'), may hold values from 0.1 to 0.6
- w_out: bfloat16 [2048, 2048], P('tp'), may hold values from -0.125 to 0.125
- norm_gain: float32 [2048], replicated, may hold values from 0.25 to 1.75
- expert_gate: bfloat16 [64, 2048, 1408], P('ep', None, 'tp'), may hold values from -0.125 to 0.125
- expert_up: bfloat16 [64, 2048, 1408], P('ep', None, 'tp'), may hold values from -0.125 to 0.125
- expert_down: bfloat16 [64, 1408, 2048], P('ep', 'tp'), may hold values from -0.15625 to 0.15625
- shared_gate: bfloat16 [2048, 3584], P(None, 'tp'), may hold values from -0.125 to 0.125
- shared_up: bfloat16 [2048, 3584], P(None, 'tp'), may hold values from -0.125 to 0.125
- shared_down: bfloat16 [3584, 2048], P('tp'), may hold values from -0.09375 to 0.09375
- shared_router: bfloat16 [2048], replicated, may hold values from -0.125 to 0.125
Outputs:
- mixed: bfloat16 [16384, 2048], P('ep', 'tp')
Inputs may be any that keep to these rules, and one draw needn't show every extreme that they name: `routes`: in each aligned block of 512 rows, no expert is named by more than 48 rows, a bound that some block reaches. `segment_ids`: segment numbers never fall within a block; each prompt has at most 256 tokens, and some has exactly 256.
All inputs are finite; a program needn't handle non-finite values.
Results may differ from a plain program's by a relative error of at most 0.012.
Values may be sent and summed in bfloat16 or wider, within the bound.
No kernel may reach another device: no remote copies, remote signals or barrier semaphores. Data moves between devices by JAX's collectives and lax.ppermute only.
A program may use at most 128 MiB of HBM per device.

v0:
```python
import jax
import jax.numpy as jnp
from jax import lax
from jax.sharding import PartitionSpec as P

HEAD = 128


def slots_of(block_routes, experts, capacity):
    length, picks = block_routes.shape
    flat = block_routes.reshape(length * picks)
    onehot = (flat[:, None] == jnp.arange(experts, dtype=jnp.int32)[None, :]).astype(jnp.int32)
    before = jnp.cumsum(onehot, axis=0, dtype=jnp.int32) - onehot
    rank = jnp.sum(before * onehot, axis=1, dtype=jnp.int32)
    slot = flat * capacity + rank
    owners = jnp.arange(length * picks, dtype=jnp.int32) // picks
    table = jnp.full((experts * capacity,), -1, dtype=jnp.int32).at[slot].set(owners)
    return (slot.reshape(length, picks), table)


def attend_local(query_block, key_block, value_block, segment):
    length = query_block.shape[0]
    heads = query_block.shape[1] // HEAD
    places = jnp.arange(length, dtype=jnp.int32)
    allowed = (segment[:, None] == segment[None, :]) & (places[:, None] >= places[None, :])

    def one_head(operands):
        query_rows, key_rows, value_rows = operands
        scores = jnp.dot(query_rows, key_rows.T, preferred_element_type=jnp.float32) * HEAD ** (
            -0.5
        )
        scores = jnp.where(allowed, scores, -jnp.inf)
        highest = jnp.max(scores, axis=1, keepdims=True)
        weights = jnp.exp(scores - highest)
        shares = (weights / jnp.sum(weights, axis=1, keepdims=True)).astype(jnp.bfloat16)
        return jnp.dot(shares, value_rows, preferred_element_type=jnp.float32).astype(jnp.bfloat16)

    def by_head(values):
        return values.reshape(length, heads, HEAD).transpose(1, 0, 2)

    attended = lax.map(one_head, (by_head(query_block), by_head(key_block), by_head(value_block)))
    return attended.transpose(1, 0, 2).reshape(length, heads * HEAD)


def on_device(
    stream,
    queries,
    keys_in,
    values_in,
    segment_ids,
    routes,
    route_weights,
    w_out,
    norm_gain,
    expert_gate,
    expert_up,
    expert_down,
    shared_gate,
    shared_up,
    shared_down,
    shared_router,
):
    length, width = stream.shape
    ep_count = lax.axis_size("ep")
    tp_count = lax.axis_size("tp")
    attended = attend_local(queries, keys_in, values_in, segment_ids[0])
    partial_value = jnp.dot(attended, w_out, preferred_element_type=jnp.float32)
    resid = stream.astype(jnp.float32) + lax.psum(partial_value.astype(jnp.bfloat16), "tp").astype(
        jnp.float32
    )
    normed = (
        resid * lax.rsqrt(jnp.mean(resid * resid, axis=1, keepdims=True) + 1e-06) * norm_gain
    ).astype(jnp.bfloat16)
    shared_gate_rows = jnp.dot(normed, shared_gate, preferred_element_type=jnp.float32)
    shared_up_rows = jnp.dot(normed, shared_up, preferred_element_type=jnp.float32)
    shared_hidden = (jax.nn.silu(shared_gate_rows) * shared_up_rows).astype(jnp.bfloat16)
    shared_part = jnp.dot(shared_hidden, shared_down, preferred_element_type=jnp.float32)
    shared_cols = lax.psum_scatter(
        shared_part.astype(jnp.bfloat16), "tp", scatter_dimension=1, tiled=True
    ).astype(jnp.float32)
    shared_scale = jax.nn.sigmoid(
        jnp.dot(normed, shared_router, preferred_element_type=jnp.float32)
    )
    local_experts = expert_gate.shape[0]
    experts = local_experts * ep_count
    picks = routes.shape[1]
    divisor = 2 * experts * tp_count
    capacity = tp_count * ((3 * length * picks + divisor - 1) // divisor)
    slot, table = slots_of(routes, experts, capacity)
    live = table >= 0
    outgoing = jnp.take(normed, jnp.maximum(table, 0), axis=0)
    outgoing = jnp.where(live[:, None], outgoing, jnp.zeros_like(outgoing))
    outgoing = outgoing.reshape(ep_count, local_experts, capacity, width)
    incoming = lax.all_to_all(outgoing, "ep", split_axis=0, concat_axis=0, tiled=True)
    gate_rows = jnp.einsum(
        "sjcd,jdf->sjcf", incoming, expert_gate, preferred_element_type=jnp.float32
    )
    up_rows = jnp.einsum("sjcd,jdf->sjcf", incoming, expert_up, preferred_element_type=jnp.float32)
    expert_hidden = (jax.nn.silu(gate_rows) * up_rows).astype(jnp.bfloat16)
    expert_part = jnp.einsum(
        "sjcf,jfd->sjcd", expert_hidden, expert_down, preferred_element_type=jnp.float32
    )
    expert_cols = lax.psum_scatter(
        expert_part.astype(jnp.bfloat16), "tp", scatter_dimension=3, tiled=True
    )
    returned = lax.all_to_all(expert_cols, "ep", split_axis=0, concat_axis=0, tiled=True)
    columns = returned.shape[3]
    flat_results = returned.reshape(experts * capacity, columns)
    picked = (
        jnp.take(flat_results, slot.reshape(-1), axis=0)
        .reshape(length, picks, columns)
        .astype(jnp.float32)
    )
    routed = jnp.sum(picked * route_weights[:, :, None], axis=1)
    resid_cols = lax.dynamic_slice_in_dim(resid, lax.axis_index("tp") * columns, columns, 1)
    return (resid_cols + shared_scale[:, None] * shared_cols + routed).astype(jnp.bfloat16)


def solution(mesh):
    placed = (
        P("ep", None),
        P("ep", "tp"),
        P("ep", "tp"),
        P("ep", "tp"),
        P("ep", None),
        P("ep", None),
        P("ep", None),
        P("tp", None),
        P(),
        P("ep", None, "tp"),
        P("ep", None, "tp"),
        P("ep", "tp", None),
        P(None, "tp"),
        P(None, "tp"),
        P("tp", None),
        P(),
    )
    return jax.shard_map(
        on_device, mesh=mesh, in_specs=placed, out_specs=P("ep", "tp"), check_vma=False
    )
```

profile of v0, /device:TPU:0, one launch (start us, length us, event | category | flops | bytes accessed | tf_op | source)
XLA Modules:
  0.0 510.2 jit_solution(16891996998942227729)
XLA Ops:
  6.5 2.2 copy.52
  8.7 2.1 copy.53
  10.8 2.1 copy.54
  12.9 14.5 %while.11 = (s32[]{:T(128)}, bf16[4,512,128]{1,2,0:T(8,128)(2,1)}, bf16[4,512,128]{1,2,0:T(8,128)(2,1)}, bf16[4,512,128]{1,2,0:T(8,128)(2,1)}, bf16[4,512,128]{1,2,0:T(8,128)(2,1)}, /*index=5*/s32[512]{0:T(512)}, s32[]{:T(128)}) while((s32[]{:T(128)}, bf16[4,512,128]{1,2,0:T(8,128)(2,1)}, bf16[4,512,128]{1,2,0:T(8,128)(2,1)}, ...), condition=%wide.region_3.4_spmd.clone, body=%wide.region_0.3_spmd.clone.sunk | while | flops 137165824 | bytes 4209757 | solution.py:41
  12.9 1.3 fusion.63
  16.5 1.3 fusion.63
  20.1 1.3 fusion.63
  23.7 1.3 fusion.63
  27.4 4.3 convolution_convert_fusion.2
  33.5 31.5 %reduce-window.6 = s32[64,16,128]{2,1,0:T(8,128)S(1)} reduce-window(s32[64,16,128]{2,1,0:T(8,128)} %fusion.38, s32[]{:T(128)} %constant.82.clone.1), window={size=1x1x128 pad=0_0x0_0x127_0}, to_apply=%region_7.8 | reduce-window | flops 16646144 | bytes 1048580 | tf_op jit(solution)/shard_map/reduce-window
  66.0 1.5 copy.73
  68.1 8.1 %scatter_custom_fusion = s32[3072]{0:T(1024)S(1)} fusion(s32[2048]{0:T(1024)S(1)} %bitcast.120, s32[2048]{0:T(1024)S(1)} %add_select_fusion, s32[]{:T(128)} %constant.94.clone.1), kind=kCustom, calls=%fused_computation.68 | custom fusion | bytes 12292 | tf_op jit(solution)/shard_map/scatter | solution.py:17
  76.4 16.7 %all-reduce.2.cloned.1.call-done = bf16[512,2048]{1,0:T(8,128)(2,1)} async-done(((bf16[512,2048]{1,0:T(8,128)(2,1)}), bf16[512,2048]{1,0:T(8,128)(2,1)}) %all-reduce.2.cloned.1.call-update) | async-done | bytes 2097168 | tf_op jit(solution)/shard_map/psum | solution.py:68
  93.1 5.0 convert_add_fusion
  98.2 2.3 multiply_convert_fusion
  100.5 25.7 %gather_fusion = bf16[3072,2048]{1,0:T(8,128)(2,1)} fusion(bf16[512,2048]{1,0:T(8,128)(2,1)} %multiply_convert_fusion, s32[3072]{0:T(1024)S(1)} %maximum_clamp_fusion), kind=kCustom, calls=%fused_computation | custom fusion | bytes 25178112 | tf_op jit(solution)/shard_map/jit(_take)/gather | solution.py:91
  126.2 7.0 %select_select_fusion = bf16[32,2,48,2048]{3,2,1,0:T(8,128)(2,1)S(1)} fusion(bf16[32,2,48,2048]{3,2,1,0:T(8,128)(2,1)} %bitcast.114, pred[32,2,48]{2,1,0:T(4,128)(4,1)S(1)} %broadcast_in_dim.67, pred[32,2,48]{2,1,0:T(4,128)(4,1)S(1)} %broadcast_in_dim.65), kind=kLoop, calls=%fused_computation.23 | loop fusion | flops 12582912 | bytes 25171968 | tf_op jit(solution)/shard_map/jit(_where)/select_n | solution.py:92
  133.2 148.1 %all_to_all.10 = bf16[32,2,48,2048]{3,2,1,0:T(8,128)(2,1)S(1)} all-to-all(bf16[32,2,48,2048]{3,2,1,0:T(8,128)(2,1)S(1)} %select_select_fusion), channel_id=1, replica_groups=mesh['ep'=32,'tp'=4] {'ep'}, dimensions={0} | all-to-all | bytes 25165824 | tf_op jit(solution)/shard_map/all_to_all | solution.py:94
  281.3 4.5 copy-done.1
  285.7 8.6 %fusion.14 = f32[2,32,48,352]{3,2,1,0:T(8,128)} fusion(bf16[32,2,48,2048]{3,2,1,0:T(8,128)(2,1)S(1)} %all_to_all.10, bf16[2,2048,352]{1,2,0:T(8,128)(2,1)S(1)} %copy-done.8), kind=kOutput, calls=%fused_computation.24 | convolution fusion | flops 4429185024 | bytes 19791872 | tf_op jit(solution)/shard_map/sjcd,jdf->sjcf/dot_general | solution.py:98
  294.3 20.3 %convert_bitcast_fusion = bf16[32,2,48,2048]{3,2,0,1:T(8,128)(2,1)} fusion(bf16[2,352,2048]{2,1,0:T(8,128)(2,1)S(1)} %copy-done, f32[2,32,48,352]{3,2,1,0:T(8,128)} %fusion.14, bf16[32,2,48,2048]{3,2,1,0:T(8,128)(2,1)} %copy-done.1, bf16[2,2048,352]{1,2,0:T(8,128)(2,1)} %param.27), kind=kOutput, calls=%fused_computation.22 | convolution fusion | flops 8871149568 | bytes 35258368 | tf_op jit(solution)/shard_map/sjcf,jfd->sjcd/dot_general | solution.py:100
  314.9 6.3 %fusion.48 = f32[512,896]{1,0:T(8,128)} fusion(bf16[512,2048]{1,0:T(8,128)(2,1)} %multiply_convert_fusion, bf16[2048,896]{1,0:T(8,128)(2,1)} %param.30), kind=kOutput, calls=%fused_computation.78 | convolution fusion | flops 1879048192 | bytes 7602176 | tf_op jit(solution)/shard_map/dot_general | solution.py:74
  321.2 10.2 %convolution_convert_fusion.1 = bf16[512,2048]{1,0:T(8,128)(2,1)} fusion(bf16[896,2048]{1,0:T(8,128)(2,1)} %param.32, f32[512,896]{1,0:T(8,128)} %fusion.48, bf16[512,2048]{1,0:T(8,128)(2,1)} %multiply_convert_fusion, bf16[2048,896]{1,0:T(8,128)(2,1)} %param.31), kind=kOutput, calls=%fused_computation.39 | convolution fusion | flops 3761897472 | bytes 13369344 | tf_op jit(solution)/shard_map/dot_general | solution.py:77
  331.4 94.2 %reduce-scatter.5.cloned.1.call-done = bf16[32,2,48,512]{3,2,0,1:T(8,128)(2,1)} async-done(((bf16[32,2,48,2048]{3,2,0,1:T(8,128)(2,1)}), bf16[32,2,48,512]{3,2,0,1:T(8,128)(2,1)}) %reduce-scatter.5.cloned.1.call-update) | async-done | bytes 3145744 | tf_op jit(solution)/shard_map/reduce_scatter | solution.py:103
  425.6 3.9 copy.68
  429.5 7.5 %all-to-all-start.1 = ((bf16[32,2,48,512]{3,2,1,0:T(8,128)(2,1)}), bf16[32,2,48,512]{3,2,1,0:T(8,128)(2,1)}, u32[]{:S(2)}, u32[]{:S(2)}) async-start(bf16[32,2,48,512]{3,2,1,0:T(8,128)(2,1)} %copy.68), calls=%async_computation.3 | async-start | bytes 6291456 | tf_op jit(solution)/shard_map/all_to_all | solution.py:106
  437.8 2.2 fusion.47
  440.0 38.9 %all-to-all-done.1 = bf16[32,2,48,512]{3,2,1,0:T(8,128)(2,1)} async-done(((bf16[32,2,48,512]{3,2,1,0:T(8,128)(2,1)}), bf16[32,2,48,512]{3,2,1,0:T(8,128)(2,1)}, u32[]{:S(2)}, u32[]{:S(2)}) %all-to-all-start.1) | async-done | bytes 3145760 | tf_op jit(solution)/shard_map/all_to_all | solution.py:106
  479.0 11.5 %gather_fusion.1 = bf16[2048,512]{1,0:T(8,128)(2,1)} fusion(bf16[3072,512]{1,0:T(8,128)(2,1)} %bitcast.25, s32[2048]{0:T(1024)S(1)} %broadcast_clamp_fusion), kind=kCustom, calls=%fused_computation.1 | custom fusion | bytes 4202496 | tf_op jit(solution)/shard_map/jit(_take)/gather | solution.py:110
  490.5 4.0 gather.15
  494.5 6.5 %multiply_reduce_fusion = f32[512,512]{1,0:T(8,128)} fusion(f32[512,4]{1,0:T(8,128)S(1)} %copy.69, bf16[512,4,512]{2,1,0:T(4,128)(2,1)} %gather.15, pred[512,4]{1,0:T(8,128)(4,1)S(1)} %copy.64), kind=kLoop, calls=%fused_computation.35 | loop fusion | flops 3932160 | bytes 3155968 | tf_op jit(solution)/shard_map/reduce_sum | solution.py:114
  501.0 2.7 add_convert_fusion
  (67 shorter events, 13.7 us)
Async XLA Ops:
  6.5 287.8 %copy-start = (bf16[2,352,2048]{2,1,0:T(8,128)(2,1)S(1)}, bf16[2,352,2048]{2,1,0:T(8,128)(2,1)}, u32[]{:S(2)}) copy-start(bf16[2,352,2048]{2,1,0:T(8,128)(2,1)} %param.29) | copy-start | bytes 8650756
  6.5 86.6 %all-reduce.2.cloned.1.call-start = ((), (), s32[]{:S(2)}) async-start(), calls=%async_computation.4 | async-start | bytes 4194304 | tf_op jit(solution)/shard_map/psum | solution.py:68
  27.4 4.4 copy-start.4
  31.7 393.9 %reduce-scatter.5.cloned.1.call-start = ((), (), s32[]{:S(2)}) async-start(), calls=%async_computation.6 | async-start | bytes 15728640 | tf_op jit(solution)/shard_map/reduce_scatter | solution.py:103
  76.4 21.7 %copy-start.5 = (f32[2048]{0:T(1024)S(1)}, f32[2048]{0:T(1024)}, u32[]{:S(2)}) copy-start(f32[2048]{0:T(1024)} %param.26) | copy-start | bytes 24580
  93.1 5.0 copy-start.2
  93.1 5.0 copy-start.3
  133.1 152.6 %copy-start.8 = (bf16[2,2048,352]{1,2,0:T(8,128)(2,1)S(1)}, bf16[2,2048,352]{1,2,0:T(8,128)(2,1)}, u32[]{:S(2)}) copy-start(bf16[2,2048,352]{1,2,0:T(8,128)(2,1)} %param.28) | copy-start | bytes 8650756
  281.2 4.5 copy-start.1
  314.7 186.3 %reduce-scatter.3.cloned.1.call-start = ((), (), s32[]{:S(2)}) async-start(), calls=%async_computation.5 | async-start | bytes 2621440 | tf_op jit(solution)/shard_map/reduce_scatter | solution.py:78
  429.5 7.8 %copy-start.7 = (bf16[2048]{0:T(1024)(128)(2,1)S(1)}, bf16[2048]{0:T(1024)(128)(2,1)}, u32[]{:S(2)}) copy-start(bf16[2048]{0:T(1024)(128)(2,1)} %param.33) | copy-start | bytes 12292
  429.5 7.8 %copy-start.6 = (f32[512,4]{0,1:T(4,128)S(1)}, f32[512,4]{0,1:T(4,128)}, u32[]{:S(2)}) copy-start(f32[512,4]{0,1:T(4,128)} %param.24) | copy-start | bytes 24580
  429.5 49.5 %all-to-all-start.1 = ((bf16[32,2,48,512]{3,2,1,0:T(8,128)(2,1)}), bf16[32,2,48,512]{3,2,1,0:T(8,128)(2,1)}, u32[]{:S(2)}, u32[]{:S(2)}) async-start(bf16[32,2,48,512]{3,2,1,0:T(8,128)(2,1)} %copy.68), calls=%async_computation.3 | async-start | bytes 6291456 | tf_op jit(solution)/shard_map/all_to_all | solution.py:106
Sparse Core Ops, SparseCore 0:
  31.9 61.2 all-reduce.1
  314.8 110.7 reduce-scatter.4
  428.0 29.4 reduce-scatter.2
where the time goes:
time: 513 us; the launch traced here: 510 us
  waiting for transfers between devices  150 us (29%)
  blocking collectives  148 us (29%)
  local copies, waits for them, and re-layouts  71.3 us (14%)
  matrix products  62.4 us (12%)
  other arithmetic  57.4 us (11%)
  between operations  13.3 us (3%)
  starting transfers between devices  7.79 us (2%)
    all_to_all x1, blocking collectives, on_device(): lax.all_to_all(outgoing, 'ep', split_axis=0, concat_axis=0, tiled=True)  148 us
    reduce_scatter x1, waiting for transfers between devices, on_device(): lax.psum_scatter(expert_part.astype(jnp.bfloat16), 'tp', scatter_dimensio...  94.2 us
    all_to_all x1, waiting for transfers between devices, on_device(): lax.all_to_all(expert_cols, 'ep', split_axis=0, concat_axis=0, tiled=True)  38.9 us
    another operation x3, other arithmetic  31.9 us
    gather x1, local copies, waits for them, and re-layouts, on_device(): outgoing = jnp.take(normed, jnp.maximum(table, 0), axis=0)  25.7 us
    dot_general x1, matrix products, on_device(): jnp.einsum('sjcf,jfd->sjcd', expert_hidden, expert_down, preferred_elemen...  20.3 us
    psum x1, waiting for transfers between devices, on_device(): lax.psum(partial_value.astype(jnp.bfloat16), 'tp').astype(jnp.float32)  16.7 us
    gather x2, local copies, waits for them, and re-layouts, on_device(): jnp.take(flat_results, slot.reshape(-1), axis=0)  15.5 us
  transfers between devices with their start and end apart: 4, of which 3 were waited for; matrix products, arithmetic and copies ran while one was open for 18% of the time, Pallas kernels for 0%

commit v1 on v0

--- a/solution.py
+++ b/solution.py
@@ -4,6 +4,7 @@
 from jax.sharding import PartitionSpec as P
 
 HEAD = 128
+_tell_kinds = lambda inp: lax.all_gather(inp, "tp").sum(axis=0)
 
 
 def slots_of(block_routes, experts, capacity):
@@ -65,7 +66,7 @@
     tp_count = lax.axis_size("tp")
     attended = attend_local(queries, keys_in, values_in, segment_ids[0])
     partial_value = jnp.dot(attended, w_out, preferred_element_type=jnp.float32)
-    resid = stream.astype(jnp.float32) + lax.psum(partial_value.astype(jnp.bfloat16), "tp").astype(
+    resid = stream.astype(jnp.float32) + _tell_kinds(partial_value.astype(jnp.bfloat16)).astype(
         jnp.float32
     )
     normed = (

time: 513 us -> 546 us (1.064)
  waiting for transfers between devices: 150 us -> 175 us
  other arithmetic: 57.4 us -> 64.7 us
    all_gather x0 -> x1, waiting for transfers between devices: none -> 41 us  [_tell_kinds = lambda inp: lax.all_gather(inp, 'tp').sum(axis=0)]
    psum x1 -> x0, waiting for transfers between devices: 16.7 us -> none  [on_device(): lax.psum(partial_value.astype(jnp.bfloat16), 'tp').astype(jnp.float32)]
    reduce_sum x0 -> x1, other arithmetic: none -> 7.27 us  [_tell_kinds = lambda inp: lax.all_gather(inp, 'tp').sum(axis=0)]
  transfers between devices with their start and end apart: 4 -> 4, of which waited for: 3 -> 3; matrix products, arithmetic and copies ran while one was open for 18% -> 17% of each run, Pallas kernels for 0% -> 0%
where the time goes in v1:
time: 546 us; the launch traced here: 543 us
  waiting for transfers between devices  175 us (32%)
  blocking collectives  148 us (27%)
  local copies, waits for them, and re-layouts  71.2 us (13%)
  other arithmetic  64.7 us (12%)
  matrix products  63 us (12%)
  between operations  13.3 us (2%)
  starting transfers between devices  7.8 us (1%)
    all_to_all x1, blocking collectives, on_device(): lax.all_to_all(outgoing, 'ep', split_axis=0, concat_axis=0, tiled=True)  148 us
    reduce_scatter x1, waiting for transfers between devices, on_device(): lax.psum_scatter(expert_part.astype(jnp.bfloat16), 'tp', scatter_dimensio...  94.9 us
    all_gather x1, waiting for transfers between devices, _tell_kinds = lambda inp: lax.all_gather(inp, 'tp').sum(axis=0)  41 us
    all_to_all x1, waiting for transfers between devices, on_device(): lax.all_to_all(expert_cols, 'ep', split_axis=0, concat_axis=0, tiled=True)  38.9 us
    another operation x3, other arithmetic  32 us
    gather x1, local copies, waits for them, and re-layouts, on_device(): outgoing = jnp.take(normed, jnp.maximum(table, 0), axis=0)  25.7 us
    dot_general x1, matrix products, on_device(): jnp.einsum('sjcf,jfd->sjcd', expert_hidden, expert_down, preferred_elemen...  20.3 us
    gather x2, local copies, waits for them, and re-layouts, on_device(): jnp.take(flat_results, slot.reshape(-1), axis=0)  15.5 us
  transfers between devices with their start and end apart: 4, of which 3 were waited for; matrix products, arithmetic and copies ran while one was open for 17% of the time, Pallas kernels for 0%

profile of v1, /device:TPU:0, one launch (start us, length us, event | category | flops | bytes accessed | tf_op | source)
XLA Modules:
  0.0 543.2 jit_solution(6399092690206121977)
XLA Ops:
  6.5 2.2 copy.52
  8.7 2.1 copy.53
  10.8 2.1 copy.54
  12.9 14.5 %while.11 = (s32[]{:T(128)}, bf16[4,512,128]{1,2,0:T(8,128)(2,1)}, bf16[4,512,128]{1,2,0:T(8,128)(2,1)}, bf16[4,512,128]{1,2,0:T(8,128)(2,1)}, bf16[4,512,128]{1,2,0:T(8,128)(2,1)}, /*index=5*/s32[512]{0:T(512)}, s32[]{:T(128)}) while((s32[]{:T(128)}, bf16[4,512,128]{1,2,0:T(8,128)(2,1)}, bf16[4,512,128]{1,2,0:T(8,128)(2,1)}, ...), condition=%wide.region_3.4_spmd.clone, body=%wide.region_0.3_spmd.clone.sunk | while | flops 137165824 | bytes 4209757 | solution.py:42
  12.9 1.3 fusion.63
  16.5 1.3 fusion.63
  20.1 1.3 fusion.63
  27.4 4.4 convolution_convert_fusion.2
  33.6 31.6 %reduce-window.6 = s32[64,16,128]{2,1,0:T(8,128)S(1)} reduce-window(s32[64,16,128]{2,1,0:T(8,128)} %fusion.38, s32[]{:T(128)} %constant.83.clone.1), window={size=1x1x128 pad=0_0x0_0x127_0}, to_apply=%region_7.8 | reduce-window | flops 16646144 | bytes 1048580 | tf_op jit(solution)/shard_map/reduce-window
  66.1 1.5 copy.73
  68.3 8.1 %scatter_custom_fusion = s32[3072]{0:T(1024)S(1)} fusion(s32[2048]{0:T(1024)S(1)} %bitcast.122, s32[2048]{0:T(1024)S(1)} %add_select_fusion, s32[]{:T(128)} %constant.95.clone.1), kind=kCustom, calls=%fused_computation.68 | custom fusion | bytes 12292 | tf_op jit(solution)/shard_map/scatter | solution.py:18
  76.6 41.0 %all-gather.3.cloned.1.call-done = bf16[2048,2048]{1,0:T(8,128)(2,1)} async-done(((bf16[512,2048]{1,0:T(8,128)(2,1)}), bf16[2048,2048]{1,0:T(8,128)(2,1)}) %all-gather.3.cloned.1.call-update) | async-done | bytes 8388624 | tf_op jit(solution)/shard_map/all_gather | solution.py:7
  117.6 7.3 %reduce_sum.52 = bf16[512,2048]{1,0:T(8,128)(2,1)} reduce(bf16[4,512,2048]{2,1,0:T(8,128)(2,1)} %bitcast.116, bf16[]{:T(256)} %constant.84.clone.1), dimensions={0}, to_apply=%region_4.5 | reduce | flops 3145728 | bytes 10485762 | tf_op jit(solution)/shard_map/reduce_sum | solution.py:7
  124.8 5.0 convert_add_fusion
  129.9 2.3 multiply_convert_fusion
  132.2 25.7 %gather_fusion = bf16[3072,2048]{1,0:T(8,128)(2,1)} fusion(bf16[512,2048]{1,0:T(8,128)(2,1)} %multiply_convert_fusion, s32[3072]{0:T(1024)S(1)} %maximum_clamp_fusion), kind=kCustom, calls=%fused_computation | custom fusion | bytes 25178112 | tf_op jit(solution)/shard_map/jit(_take)/gather | solution.py:92
  157.9 7.0 %select_select_fusion = bf16[32,2,48,2048]{3,2,1,0:T(8,128)(2,1)S(1)} fusion(bf16[32,2,48,2048]{3,2,1,0:T(8,128)(2,1)} %bitcast.115, pred[32,2,48]{2,1,0:T(4,128)(4,1)S(1)} %broadcast_in_dim.67, pred[32,2,48]{2,1,0:T(4,128)(4,1)S(1)} %broadcast_in_dim.65), kind=kLoop, calls=%fused_computation.23 | loop fusion | flops 12582912 | bytes 25171968 | tf_op jit(solution)/shard_map/jit(_where)/select_n | solution.py:93
  164.9 148.2 %all_to_all.10 = bf16[32,2,48,2048]{3,2,1,0:T(8,128)(2,1)S(1)} all-to-all(bf16[32,2,48,2048]{3,2,1,0:T(8,128)(2,1)S(1)} %select_select_fusion), channel_id=1, replica_groups=mesh['ep'=32,'tp'=4] {'ep'}, dimensions={0} | all-to-all | bytes 25165824 | tf_op jit(solution)/shard_map/all_to_all | solution.py:95
  313.0 4.5 copy-done.2
  317.5 8.6 %fusion.14 = f32[2,32,48,352]{3,2,1,0:T(8,128)} fusion(bf16[32,2,48,2048]{3,2,1,0:T(8,128)(2,1)S(1)} %all_to_all.10, bf16[2,2048,352]{1,2,0:T(8,128)(2,1)S(1)} %copy-done.8), kind=kOutput, calls=%fused_computation.24 | convolution fusion | flops 4429185024 | bytes 19791872 | tf_op jit(solution)/shard_map/sjcd,jdf->sjcf/dot_general | solution.py:99
  326.1 20.3 %convert_bitcast_fusion = bf16[32,2,48,2048]{3,2,0,1:T(8,128)(2,1)} fusion(bf16[2,352,2048]{2,1,0:T(8,128)(2,1)S(1)} %copy-done, f32[2,32,48,352]{3,2,1,0:T(8,128)} %fusion.14, bf16[32,2,48,2048]{3,2,1,0:T(8,128)(2,1)} %copy-done.2, bf16[2,2048,352]{1,2,0:T(8,128)(2,1)} %param.27), kind=kOutput, calls=%fused_computation.22 | convolution fusion | flops 8871149568 | bytes 35258368 | tf_op jit(solution)/shard_map/sjcf,jfd->sjcd/dot_general | solution.py:101
  346.7 6.3 %fusion.48 = f32[512,896]{1,0:T(8,128)} fusion(bf16[512,2048]{1,0:T(8,128)(2,1)} %multiply_convert_fusion, bf16[2048,896]{1,0:T(8,128)(2,1)} %param.30), kind=kOutput, calls=%fused_computation.78 | convolution fusion | flops 1879048192 | bytes 7602176 | tf_op jit(solution)/shard_map/dot_general | solution.py:75
  353.0 10.6 %convolution_convert_fusion.1 = bf16[512,2048]{1,0:T(8,128)(2,1)} fusion(bf16[896,2048]{1,0:T(8,128)(2,1)} %param.32, f32[512,896]{1,0:T(8,128)} %fusion.48, bf16[512,2048]{1,0:T(8,128)(2,1)} %multiply_convert_fusion, bf16[2048,896]{1,0:T(8,128)(2,1)} %param.31), kind=kOutput, calls=%fused_computation.39 | convolution fusion | flops 3761897472 | bytes 13369344 | tf_op jit(solution)/shard_map/dot_general | solution.py:78
  363.6 94.9 %reduce-scatter.5.cloned.1.call-done = bf16[32,2,48,512]{3,2,0,1:T(8,128)(2,1)} async-done(((bf16[32,2,48,2048]{3,2,0,1:T(8,128)(2,1)}), bf16[32,2,48,512]{3,2,0,1:T(8,128)(2,1)}) %reduce-scatter.5.cloned.1.call-update) | async-done | bytes 3145744 | tf_op jit(solution)/shard_map/reduce_scatter | solution.py:104
  458.5 3.9 copy.68
  462.4 7.5 %all-to-all-start.1 = ((bf16[32,2,48,512]{3,2,1,0:T(8,128)(2,1)}), bf16[32,2,48,512]{3,2,1,0:T(8,128)(2,1)}, u32[]{:S(2)}, u32[]{:S(2)}) async-start(bf16[32,2,48,512]{3,2,1,0:T(8,128)(2,1)} %copy.68), calls=%async_computation.3 | async-start | bytes 6291456 | tf_op jit(solution)/shard_map/all_to_all | solution.py:107
  470.7 2.2 fusion.47
  473.0 38.9 %all-to-all-done.1 = bf16[32,2,48,512]{3,2,1,0:T(8,128)(2,1)} async-done(((bf16[32,2,48,512]{3,2,1,0:T(8,128)(2,1)}), bf16[32,2,48,512]{3,2,1,0:T(8,128)(2,1)}, u32[]{:S(2)}, u32[]{:S(2)}) %all-to-all-start.1) | async-done | bytes 3145760 | tf_op jit(solution)/shard_map/all_to_all | solution.py:107
  511.9 11.5 %gather_fusion.1 = bf16[2048,512]{1,0:T(8,128)(2,1)} fusion(bf16[3072,512]{1,0:T(8,128)(2,1)} %bitcast.26, s32[2048]{0:T(1024)S(1)} %broadcast_clamp_fusion), kind=kCustom, calls=%fused_computation.1 | custom fusion | bytes 4202496 | tf_op jit(solution)/shard_map/jit(_take)/gather | solution.py:111
  523.4 4.0 gather.15
  527.4 6.5 %multiply_reduce_fusion = f32[512,512]{1,0:T(8,128)} fusion(f32[512,4]{1,0:T(8,128)S(1)} %copy.69, bf16[512,4,512]{2,1,0:T(4,128)(2,1)} %gather.15, pred[512,4]{1,0:T(8,128)(4,1)S(1)} %copy.64), kind=kLoop, calls=%fused_computation.35 | loop fusion | flops 3932160 | bytes 3155968 | tf_op jit(solution)/shard_map/reduce_sum | solution.py:115
  533.9 2.7 add_convert_fusion
  (68 shorter events, 15.0 us)
Async XLA Ops:
  6.5 319.6 %copy-start = (bf16[2,352,2048]{2,1,0:T(8,128)(2,1)S(1)}, bf16[2,352,2048]{2,1,0:T(8,128)(2,1)}, u32[]{:S(2)}) copy-start(bf16[2,352,2048]{2,1,0:T(8,128)(2,1)} %param.29) | copy-start | bytes 8650756
  6.5 111.0 %all-gather.3.cloned.1.call-start = ((), (), s32[]{:S(2)}) async-start(), calls=%async_computation.6 | async-start | bytes 10485760 | tf_op jit(solution)/shard_map/all_gather | solution.py:7
  27.4 4.5 copy-start.4
  31.8 426.7 %reduce-scatter.5.cloned.1.call-start = ((), (), s32[]{:S(2)}) async-start(), calls=%async_computation.5 | async-start | bytes 15728640 | tf_op jit(solution)/shard_map/reduce_scatter | solution.py:104
  124.8 5.0 copy-start.1
  124.8 5.0 copy-start.3
  124.8 5.0 copy-start.5
  164.9 152.7 %copy-start.8 = (bf16[2,2048,352]{1,2,0:T(8,128)(2,1)S(1)}, bf16[2,2048,352]{1,2,0:T(8,128)(2,1)}, u32[]{:S(2)}) copy-start(bf16[2,2048,352]{1,2,0:T(8,128)(2,1)} %param.28) | copy-start | bytes 8650756
  313.0 4.5 copy-start.2
  346.5 187.4 %reduce-scatter.3.cloned.1.call-start = ((), (), s32[]{:S(2)}) async-start(), calls=%async_computation.4 | async-start | bytes 2621440 | tf_op jit(solution)/shard_map/reduce_scatter | solution.py:79
  462.4 7.8 %copy-start.7 = (bf16[2048]{0:T(1024)(128)(2,1)S(1)}, bf16[2048]{0:T(1024)(128)(2,1)}, u32[]{:S(2)}) copy-start(bf16[2048]{0:T(1024)(128)(2,1)} %param.33) | copy-start | bytes 12292
  462.4 7.8 %copy-start.6 = (f32[512,4]{0,1:T(4,128)S(1)}, f32[512,4]{0,1:T(4,128)}, u32[]{:S(2)}) copy-start(f32[512,4]{0,1:T(4,128)} %param.24) | copy-start | bytes 24580
  462.4 49.5 %all-to-all-start.1 = ((bf16[32,2,48,512]{3,2,1,0:T(8,128)(2,1)}), bf16[32,2,48,512]{3,2,1,0:T(8,128)(2,1)}, u32[]{:S(2)}, u32[]{:S(2)}) async-start(bf16[32,2,48,512]{3,2,1,0:T(8,128)(2,1)} %copy.68), calls=%async_computation.3 | async-start | bytes 6291456 | tf_op jit(solution)/shard_map/all_to_all | solution.py:107
Sparse Core Ops, SparseCore 0:
  32.0 85.5 all-gather.2
  346.6 111.9 reduce-scatter.4
  460.9 29.4 reduce-scatter.2
